TPU v7x, 32 devices: a whole 2x2x4 slice. The times are simulated.
32 devices in a mesh: energy: 4 (over z), atom: 8 (over y, x, core).
Axes of the slice: x: 2, y: 2, z: 4, core: 2. Of those that a mesh axis runs over, the one named last changes fastest.
Arguments:
- t_mats: bfloat16 [4, 16, 2048], P('energy', 'atom'), may hold values from -0.75 to 0.75
- struct_table: bfloat16 [4, 64, 2048], P('energy'), may hold values from -0.359375 to 0.359375
- zone_atoms: int32 [16, 64], P('atom'), may hold values from 0 to 15, as said below
- zone_size: int32 [16], P('atom'), may hold values from 32 to 64
- pair_index: int32 [16, 384], P('atom'), may hold values from 0 to 63
- zone_link: int32 [16, 384], P('atom'), may hold values from 0 to 63
- weights: float32 [4, 2], P('energy'), may hold values from -1 to 1
Outputs:
- green: float32 [16, 2048], P('atom')
Inputs may be any that keep to these rules, and one draw needn't show every extreme that they name: Atom g is owned by index g // 2 of the atom axis; zone_atoms[g, 0] is g; the owner of every member of atom g's zone lies -4 to 3 steps from g's owner along the atom axis, counted around the axis, and both extreme offsets occur in every zone; members may repeat (periodic images).
All inputs are finite; a program needn't handle non-finite values.
Results may differ from a plain program's by a relative error of at most 0.003.
Values may be sent and summed in bfloat16 or wider, within the bound.
No kernel may reach another device: no remote copies, remote signals or barrier semaphores. Data moves between devices by JAX's collectives and lax.ppermute only.
A program may use at most 128 MiB of HBM per device.

v0:
```python
import jax
import jax.numpy as jnp
from jax import lax
from jax.sharding import PartitionSpec as P

L = 32
Z = 64
NB = 6
ITERS = 3


def real_form(block):
    parts = block.reshape(block.shape[:-1] + (2, L, L))
    real_part = parts[..., 0, :, :]
    imag_part = parts[..., 1, :, :]
    top_rows = jnp.concatenate([real_part, -imag_part], axis=-1)
    bottom_rows = jnp.concatenate([imag_part, real_part], axis=-1)
    return jnp.concatenate([top_rows, bottom_rows], axis=-2)


def scatter_terms(couplings, gathered, pattern):
    products = jnp.einsum(pattern, couplings, gathered, preferred_element_type=jnp.float32)
    real_part = products[..., 0, 0, :, :] - products[..., 1, 1, :, :]
    imag_part = products[..., 1, 0, :, :] + products[..., 0, 1, :, :]
    return jnp.concatenate([real_part, imag_part], axis=-2)


def take_links(column_parts, link_rows):
    return jax.vmap(
        lambda member_col, member_links: member_col[:, member_links], in_axes=(1, 0), out_axes=1
    )(column_parts, link_rows)


def solve_zones(zone_block, couplings_flat, links):
    e_dev, a_dev = (zone_block.shape[0], zone_block.shape[1])
    t_real = real_form(zone_block)
    couplings = couplings_flat.reshape(e_dev, a_dev, Z, NB, 2, L, L)
    start_block = t_real[:, :, 0, :, :L].astype(jnp.float32)
    start = jnp.zeros((e_dev, a_dev, Z, 2 * L, L), jnp.float32).at[:, :, 0].set(start_block)
    column = start
    for repeat in range(ITERS - 1):
        column_parts = column.astype(jnp.bfloat16).reshape(e_dev, a_dev, Z, 2, L, L)
        gathered = take_links(column_parts, links).reshape(e_dev, a_dev, Z, NB, 2, L, L)
        coupled = scatter_terms(couplings, gathered, "eganpij,eganqjk->egapqik").astype(
            jnp.bfloat16
        )
        column = (
            jnp.einsum("egaij,egajk->egaik", t_real, coupled, preferred_element_type=jnp.float32)
            + start
        )
    column_parts = column.astype(jnp.bfloat16).reshape(e_dev, a_dev, Z, 2, L, L)
    gathered = take_links(column_parts, links[:, :NB])
    coupled = scatter_terms(couplings[:, :, 0], gathered, "egnpij,egnqjk->egpqik").astype(
        jnp.bfloat16
    )
    return (
        jnp.einsum("egij,egjk->egik", t_real[:, :, 0], coupled, preferred_element_type=jnp.float32)
        + start_block
    )


def body(t_mats, struct_table, zone_atoms, zone_size, pair_index, zone_link, weights):
    e_dev, a_dev, block_flat = t_mats.shape
    window = lax.all_gather(t_mats, "atom", axis=1, tiled=True)
    present = jnp.arange(Z, dtype=jnp.int32)[None, :] < zone_size[:, None]
    zone_block = jnp.where(
        present[None, :, :, None], window[:, zone_atoms], jnp.zeros((), jnp.bfloat16)
    )
    couplings_flat = struct_table[:, pair_index]
    diagonal = solve_zones(zone_block, couplings_flat, zone_link)
    real_rows = diagonal[:, :, :L, :].reshape(e_dev, a_dev, L * L)
    imag_rows = diagonal[:, :, L:, :].reshape(e_dev, a_dev, L * L)
    w_real = weights[:, 0][:, None, None]
    w_imag = weights[:, 1][:, None, None]
    green_real = jnp.sum(w_real * real_rows - w_imag * imag_rows, axis=0)
    green_imag = jnp.sum(w_real * imag_rows + w_imag * real_rows, axis=0)
    local_green = jnp.concatenate([green_real, green_imag], axis=-1)
    return lax.psum(local_green, "energy")


def solution(mesh):
    return jax.shard_map(
        body,
        mesh=mesh,
        in_specs=(
            P("energy", "atom", None),
            P("energy", None, None),
            P("atom", None),
            P("atom"),
            P("atom", None),
            P("atom", None),
            P("energy", None),
        ),
        out_specs=P("atom", None),
        check_vma=False,
    )
```

profile of v0, /device:TPU:0, one launch (start us, length us, event | category | flops | bytes accessed | tf_op | source)
XLA Modules:
  0.0 153.0 jit_solution(8475652753170242469)
XLA Ops:
  0.0 0.8 copy.91
  0.8 10.7 %all_gather.3 = bf16[1,16,2048]{2,0,1:T(2,128)(2,1)S(1)} all-gather(bf16[1,2,2048]{2,0,1:T(2,128)(2,1)S(1)} %copy.91), channel_id=1, replica_groups=mesh['energy'=4,'atom'=8] {'atom'}, dimensions={1}, use_global_device_ids=true | all-gather | bytes 73728 | tf_op jit(solution)/shard_map/all_gather | solution.py:64
  11.5 0.7 compare_select_fusion.3
  12.2 0.1 reshape.287
  12.3 0.9 gather_fusion
  13.2 0.3 copy.92
  13.5 0.4 gather.18
  13.9 2.0 %copy.93 = bf16[1,2,64,2,32,32]{5,4,2,1,3,0:T(8,128)(2,1)S(1)} copy(bf16[1,2,64,2,32,32]{2,1,5,4,3,0:T(2,128)(2,1)S(1)} %gather.18) | data formatting | bytes 1048576 | tf_op jit(solution)/shard_map/gather | solution.py:67
  15.9 0.1 iota_compare_fusion
  15.9 0.2 broadcast_select_fusion
  16.2 0.4 slice_bitcast_fusion.4
  16.6 0.1 fusion.57
  16.7 1.2 maximum_maximum_fusion
  17.9 0.5 scatter.9
  18.4 0.8 copy-done.4
  19.3 9.2 %gather_fusion.2 = bf16[768,2,32,32]{3,2,1,0:T(8,128)(2,1)} fusion(bf16[2,64,2,32,32]{4,3,2,1,0:T(8,128)(2,1)S(1)} %bitcast.153, s32[768]{0:T(1024)S(1)} %reshape.305), kind=kCustom, calls=%fused_computation.2 | custom fusion | bytes 6297600 | tf_op jit(solution)/shard_map/vmap()/gather | solution.py:30
  28.5 3.4 %gather_fusion.1 = bf16[768,2048]{1,0:T(8,128)(2,1)S(1)} fusion(bf16[64,2048]{1,0:T(8,128)(2,1)S(1)} %bitcast.151, s32[1024]{0:T(1024)S(1)} %pad_clamp_fusion), kind=kCustom, calls=%fused_computation.1 | custom fusion | bytes 6294528 | tf_op jit(solution)/shard_map/gather | solution.py:69
  31.9 11.8 %reshape.277 = bf16[2,64,6,2,32,32]{5,4,3,2,1,0:T(8,128)(2,1)} reshape(bf16[768,2048]{1,0:T(8,128)(2,1)S(1)} %gather_fusion.1) | data formatting | bytes 6291456 | tf_op jit(solution)/shard_map/reshape.48
  43.7 17.2 %fusion.6 = f32[1,2,64,2,2,32,32]{5,6,3,4,2,1,0:T(8,128)} fusion(bf16[2,64,6,2,32,32,1]{5,4,3,2,1,0,6:T(8,128)(2,1)} %bitcast.155, bf16[2,64,6,2,32,32]{5,4,3,2,1,0:T(8,128)(2,1)} %reshape.277), kind=kOutput, calls=%fused_computation.11 | convolution fusion | flops 201326592 | bytes 8388608 | tf_op jit(solution)/shard_map/eganpij,eganqjk->egapqik/dot_general | solution.py:22
  60.9 2.7 %fusion.27 = bf16[2,64,32,32]{2,3,1,0:T(8,128)(2,1)S(1)} fusion(f32[1,2,64,2,2,32,32]{5,6,3,4,2,1,0:T(8,128)} %fusion.6), kind=kLoop, calls=%fused_computation.34 | loop fusion | flops 262144 | bytes 1310720 | tf_op jit(solution)/shard_map/sub | solution.py:23
  63.7 2.9 %fusion.28 = bf16[2,64,32,32]{2,3,1,0:T(8,128)(2,1)S(1)} fusion(f32[1,2,64,2,2,32,32]{5,6,3,4,2,1,0:T(8,128)} %fusion.6), kind=kLoop, calls=%fused_computation.35 | loop fusion | flops 262144 | bytes 1310720 | tf_op jit(solution)/shard_map/add | solution.py:24
  66.6 1.3 fusion.24
  67.9 1.3 copy-done.7
  69.2 0.1 copy.140
  69.4 0.6 constant_dynamic-update-slice_fusion.1
  70.0 1.8 %convert_element_type.37 = bf16[1,2,64,64,32]{3,4,2,1,0:T(8,128)(2,1)S(1)} convert(f32[1,2,64,64,32]{3,4,2,1,0:T(8,128)} %constant_dynamic-update-slice_fusion.1) | non-fusion elementwise | flops 262144 | bytes 1572864 | tf_op jit(solution)/shard_map/convert_element_type | solution.py:42
  71.8 1.2 copy.129
  73.0 9.4 %gather_fusion.3 = bf16[768,2,32,32]{3,2,1,0:T(8,128)(2,1)} fusion(bf16[2,64,2,32,32]{4,3,2,1,0:T(8,128)(2,1)S(1)} %bitcast.154, s32[768]{0:T(1024)S(1)} %reshape.305), kind=kCustom, calls=%fused_computation.3 | custom fusion | bytes 6297600 | tf_op jit(solution)/shard_map/vmap()/gather | solution.py:30
  82.4 17.2 %fusion.11 = f32[1,2,64,2,2,32,32]{5,6,3,4,2,1,0:T(8,128)} fusion(bf16[2,64,6,2,32,32,1]{5,4,3,2,1,0,6:T(8,128)(2,1)} %bitcast.156, bf16[2,64,6,2,32,32]{5,4,3,2,1,0:T(8,128)(2,1)} %reshape.277), kind=kOutput, calls=%fused_computation.12 | convolution fusion | flops 201326592 | bytes 8388608 | tf_op jit(solution)/shard_map/eganpij,eganqjk->egapqik/dot_general | solution.py:22
  99.6 2.7 %fusion.29 = bf16[2,64,32,32]{2,3,1,0:T(8,128)(2,1)S(1)} fusion(f32[1,2,64,2,2,32,32]{5,6,3,4,2,1,0:T(8,128)} %fusion.11), kind=kLoop, calls=%fused_computation.36 | loop fusion | flops 262144 | bytes 1310720 | tf_op jit(solution)/shard_map/sub | solution.py:23
  102.3 2.9 %fusion.30 = bf16[2,64,32,32]{2,3,1,0:T(8,128)(2,1)S(1)} fusion(f32[1,2,64,2,2,32,32]{5,6,3,4,2,1,0:T(8,128)} %fusion.11), kind=kLoop, calls=%fused_computation.37 | loop fusion | flops 262144 | bytes 1310720 | tf_op jit(solution)/shard_map/add | solution.py:24
  105.2 1.3 fusion.22
  106.5 1.3 copy-done.8
  107.8 0.1 copy.143
  107.9 0.1 copy.107
  108.0 0.6 constant_dynamic-update-slice_fusion
  108.6 2.8 %convert_element_type.38 = bf16[1,2,64,64,32]{3,4,2,1,0:T(8,128)(2,1)} convert(f32[1,2,64,64,32]{3,4,2,1,0:T(8,128)} %constant_dynamic-update-slice_fusion) | non-fusion elementwise | flops 262144 | bytes 1572864 | tf_op jit(solution)/shard_map/convert_element_type | solution.py:51
  111.4 2.9 %copy.134 = bf16[1,2,64,64,32]{4,3,2,1,0:T(8,128)(2,1)} copy(bf16[1,2,64,64,32]{3,4,2,1,0:T(8,128)(2,1)} %convert_element_type.38) | data formatting | bytes 1048576 | tf_op jit(solution)/shard_map/vmap()/transpose;reshape | solution.py:30
  114.3 0.1 reshape.321
  114.4 2.9 %gather_fusion.4 = bf16[12,2,32,32]{3,2,1,0:T(8,128)(2,1)} fusion(bf16[2,64,2,32,32]{4,3,2,1,0:T(8,128)(2,1)} %bitcast.159, s32[12]{0:T(128)S(1)} %reshape.321), kind=kCustom, calls=%fused_computation.4 | custom fusion | bytes 98400 | tf_op jit(solution)/shard_map/vmap()/gather | solution.py:30
  117.4 11.6 %reshape.280 = bf16[1,2,64,6,2,32,32]{6,5,4,3,2,1,0:T(8,128)(2,1)} reshape(bf16[768,2048]{1,0:T(8,128)(2,1)S(1)} %copy-done.3) | data formatting | bytes 6291456 | tf_op jit(solution)/shard_map/reshape | solution.py:37
  129.0 1.3 convolution_bitcast_fusion
  130.3 1.0 fusion.26
  131.4 0.6 fusion.58
  132.0 1.2 multiply_subtract_fusion
  133.2 0.1 add.92
  133.3 0.1 sub.43
  133.4 19.6 %psum.7 = f32[2,2048]{1,0:T(2,128)} all-reduce(f32[2,2048]{1,0:T(2,128)S(1)} %pad_maximum_fusion), channel_id=1, replica_groups=mesh['energy'=4,'atom'=8] {'energy'}, use_global_device_ids=true, to_apply=%region_0.1 | all-reduce | flops 4096 | bytes 32768 | tf_op jit(solution)/shard_map/psum | solution.py:78
  (40 shorter events, 0.3 us)
Async XLA Ops:
  0.0 28.5 %copy-start = (bf16[1,64,2048]{2,1,0:T(8,128)(2,1)S(1)}, bf16[1,64,2048]{2,1,0:T(8,128)(2,1)}, u32[]{:S(2)}) copy-start(bf16[1,64,2048]{2,1,0:T(8,128)(2,1)} %param.10) | copy-start | bytes 786436
  13.5 2.4 %copy-start.12 = (s32[2]{0:T(128)S(1)}, s32[2]{0:T(128)}, u32[]{:S(2)}) copy-start(s32[2]{0:T(128)} %param.12) | copy-start | bytes 28
  17.9 1.4 copy-start.4
  17.9 1.4 copy-start.9
  19.3 9.2 %copy-start.10 = (s32[2,384]{1,0:T(2,128)S(1)}, s32[2,384]{1,0:T(2,128)}, u32[]{:S(2)}) copy-start(s32[2,384]{1,0:T(2,128)} %param.13) | copy-start | bytes 9220
  31.9 11.8 %copy-start.2 = (bf16[768,2048]{1,0:T(8,128)(2,1)}, bf16[768,2048]{1,0:T(8,128)(2,1)S(1)}, u32[]{:S(2)}) copy-start(bf16[768,2048]{1,0:T(8,128)(2,1)S(1)} %gather_fusion.1) | copy-start | bytes 9437188
  63.7 2.9 %copy-start.5 = (bf16[1,2,64,64,64]{4,3,2,1,0:T(8,128)(2,1)S(1)}, bf16[1,2,64,64,64]{4,3,2,1,0:T(8,128)(2,1)}, u32[]{:S(2)}) copy-start(bf16[1,2,64,64,64]{4,3,2,1,0:T(8,128)(2,1)} %copy-done.4) | copy-start | bytes 3145732
  67.9 1.3 copy-start.7
  102.3 2.9 %copy-start.6 = (bf16[1,2,64,64,64]{4,3,2,1,0:T(8,128)(2,1)S(1)}, bf16[1,2,64,64,64]{4,3,2,1,0:T(8,128)(2,1)}, u32[]{:S(2)}) copy-start(bf16[1,2,64,64,64]{4,3,2,1,0:T(8,128)(2,1)} %copy-done.4) | copy-start | bytes 3145732
  106.5 1.3 copy-start.8
  111.4 5.9 %copy-start.3 = (bf16[768,2048]{1,0:T(8,128)(2,1)S(1)}, bf16[768,2048]{1,0:T(8,128)(2,1)}, u32[]{:S(2)}) copy-start(bf16[768,2048]{1,0:T(8,128)(2,1)} %copy-done.2) | copy-start | bytes 9437188
  117.3 14.0 %copy-start.11 = (f32[1,2]{1,0:T(1,128)S(1)}, f32[1,2]{1,0:T(1,128)}, u32[]{:S(2)}) copy-start(f32[1,2]{1,0:T(1,128)} %param.15) | copy-start | bytes 28
  117.3 35.6 %copy-start.1 = (bf16[1,64,2048]{2,1,0:T(8,128)(2,1)S(1)}, bf16[1,64,2048]{2,1,0:T(8,128)(2,1)}, u32[]{:S(2)}) copy-start(bf16[1,64,2048]{2,1,0:T(8,128)(2,1)} %param.10) | copy-start | bytes 786436
where the time goes:
time: 153 us
  local copies, waits for them, and re-layouts  63.7 us (42%)
  matrix products  39.3 us (26%)
  blocking collectives  30.3 us (20%)
  other arithmetic  19.4 us (13%)
    dot_general x3, matrix products, scatter_terms(): jnp.einsum(pattern, couplings, gathered, preferred_element_type=jnp.float32)  35.7 us
    gather x5, local copies, waits for them, and re-layouts, take_links(): member_col[:, member_links]  21.5 us
    psum x1, blocking collectives, body(): return lax.psum(local_green, 'energy')  19.6 us
    another operation x3, local copies, waits for them, and re-layouts  11.8 us
    reshape x1, local copies, waits for them, and re-layouts, solve_zones(): couplings = couplings_flat.reshape(e_dev, a_dev, Z, NB, 2, L, L)  11.6 us
    all_gather x1, blocking collectives, body(): window = lax.all_gather(t_mats, 'atom', axis=1, tiled=True)  10.7 us
    add x3, other arithmetic, scatter_terms(): imag_part = products[..., 1, 0, :, :] + products[..., 0, 1, :, :]  5.8 us
    sub x3, other arithmetic, scatter_terms(): real_part = products[..., 0, 0, :, :] - products[..., 1, 1, :, :]  5.49 us

commit v1 on v0

v1 whole, which is shorter than its diff:
```python
import jax
import jax.numpy as jnp
from jax import lax
from jax.sharding import PartitionSpec as P

L = 32
Z = 64
NB = 6


def real_form(block):
    parts = block.reshape(block.shape[:-1] + (2, L, L))
    real_part = parts[..., 0, :, :]
    imag_part = parts[..., 1, :, :]
    top_rows = jnp.concatenate([real_part, -imag_part], axis=-1)
    bottom_rows = jnp.concatenate([imag_part, real_part], axis=-1)
    return jnp.concatenate([top_rows, bottom_rows], axis=-2)


def take_rows(table, index):
    a_dev = index.shape[0]
    return jnp.take_along_axis(table, index.reshape(a_dev, -1), axis=1).reshape(index.shape)


def body(t_mats, struct_table, zone_atoms, zone_size, pair_index, zone_link, weights):
    e_dev, a_dev, block_flat = t_mats.shape
    window = lax.all_gather(t_mats, "atom", axis=1, tiled=True)

    coupling = jnp.arange(NB, dtype=jnp.int32)
    s2 = zone_link[:, :NB]
    s1 = take_rows(zone_link, s2[:, :, None] * NB + coupling)
    n1 = NB * NB
    slots = jnp.concatenate(
        [s1.reshape(a_dev, n1), s2, jnp.zeros((a_dev, 1), jnp.int32)], axis=1
    )
    spots = slots[:, :, None] * NB + coupling
    pairs = take_rows(pair_index, spots)
    links = take_rows(zone_link, spots)
    members = take_rows(zone_atoms, slots)
    present = slots < zone_size[:, None]

    t_block = jnp.where(
        present[None, :, :, None], window[:, members], jnp.zeros((), jnp.bfloat16)
    )
    t_real = real_form(t_block)
    g_real = real_form(struct_table[:, pairs])
    start_b = real_form(t_mats)[..., :L]
    start_f = start_b.astype(jnp.float32)
    is_zero = (slots == 0)[None, :, :, None, None]

    p1 = jnp.einsum(
        "easkij,eajc->easkic", g_real[:, :, :n1], start_b, preferred_element_type=jnp.float32
    )
    hit = (links[:, :n1] == 0)[None, :, :, :, None, None]
    coupled1 = jnp.sum(jnp.where(hit, p1, 0.0), axis=3).astype(jnp.bfloat16)
    col1 = jnp.einsum(
        "easij,easjc->easic", t_real[:, :, :n1], coupled1, preferred_element_type=jnp.float32
    ) + jnp.where(is_zero[:, :, :n1], start_f[:, :, None], 0.0)
    near2 = col1.astype(jnp.bfloat16).reshape(e_dev, a_dev, NB, NB, 2 * L, L)

    g2 = g_real[:, :, n1 : n1 + NB]
    coupled2 = jnp.einsum(
        "eamnij,eamnjc->eamic", g2, near2, preferred_element_type=jnp.float32
    ).astype(jnp.bfloat16)
    col2 = jnp.einsum(
        "eamij,eamjc->eamic", t_real[:, :, n1 : n1 + NB], coupled2,
        preferred_element_type=jnp.float32,
    ) + jnp.where(is_zero[:, :, n1 : n1 + NB], start_f[:, :, None], 0.0)
    near3 = col2.astype(jnp.bfloat16)

    coupled3 = jnp.einsum(
        "eanij,eanjc->eaic", g_real[:, :, n1 + NB], near3, preferred_element_type=jnp.float32
    ).astype(jnp.bfloat16)
    diagonal = jnp.einsum(
        "eaij,eajc->eaic", t_real[:, :, n1 + NB], coupled3, preferred_element_type=jnp.float32
    ) + start_f

    real_rows = diagonal[:, :, :L, :].reshape(e_dev, a_dev, L * L)
    imag_rows = diagonal[:, :, L:, :].reshape(e_dev, a_dev, L * L)
    w_real = weights[:, 0][:, None, None]
    w_imag = weights[:, 1][:, None, None]
    green_real = jnp.sum(w_real * real_rows - w_imag * imag_rows, axis=0)
    green_imag = jnp.sum(w_real * imag_rows + w_imag * real_rows, axis=0)
    local_green = jnp.concatenate([green_real, green_imag], axis=-1)
    return lax.psum(local_green, "energy")


def solution(mesh):
    return jax.shard_map(
        body,
        mesh=mesh,
        in_specs=(
            P("energy", "atom", None),
            P("energy", None, None),
            P("atom", None),
            P("atom"),
            P("atom", None),
            P("atom", None),
            P("energy", None),
        ),
        out_specs=P("atom", None),
        check_vma=False,
    )
```

time: 153 us -> 101 us (0.66)
  matrix products: 39.3 us -> 12.9 us
  other arithmetic: 19.4 us -> 5.4 us
  local copies, waits for them, and re-layouts: 63.7 us -> 51.6 us
    dot_general x6 -> x5, matrix products: 39.3 us -> 12.9 us  [the longest x1 9.49 us: body(): jnp.einsum('easkij,eajc->easkic', g_real[:, :, :n1], start_b, preferred_e...]
    another operation x5 -> x0, local copies, waits for them, and re-layouts: 15.9 us -> none
    squeeze x1 -> x2, local copies, waits for them, and re-layouts: 0.4 us -> 7.6 us  [real_form(): imag_part = parts[..., 1, :, :]]
    add x3 -> x0, other arithmetic: 5.8 us -> none  [scatter_terms(): imag_part = products[..., 1, 0, :, :] + products[..., 0, 1, :, :]]
    sub x3 -> x0, other arithmetic: 5.49 us -> none  [scatter_terms(): real_part = products[..., 0, 0, :, :] - products[..., 1, 1, :, :]]
    convert_element_type x2 -> x0, other arithmetic: 4.6 us -> none  [solve_zones(): column_parts = column.astype(jnp.bfloat16).reshape(e_dev, a_dev, Z, 2, L, L)]
    neg x1 -> x3, other arithmetic: 0.14 us -> 2.61 us  [real_form(): top_rows = jnp.concatenate([real_part, -imag_part], axis=-1)]
    reshape x1 -> x4, local copies, waits for them, and re-layouts: 11.6 us -> 9.65 us  [the longest x2 9.42 us: real_form(): parts = block.reshape(block.shape[:-1] + (2, L, L))]
where the time goes in v1:
time: 101 us; the launch traced here: 100 us
  local copies, waits for them, and re-layouts  51.6 us (51%)
  blocking collectives  30.3 us (30%)
  matrix products  12.9 us (13%)
  other arithmetic  5.4 us (5%)
    gather x11, local copies, waits for them, and re-layouts, take_rows(): jnp.take_along_axis(table, index.reshape(a_dev, -1), axis=1)  22.1 us
    psum x1, blocking collectives, body(): return lax.psum(local_green, 'energy')  19.6 us
    all_gather x1, blocking collectives, body(): window = lax.all_gather(t_mats, 'atom', axis=1, tiled=True)  10.7 us
    dot_general x1, matrix products, body(): jnp.einsum('easkij,eajc->easkic', g_real[:, :, :n1], start_b, preferred_e...  9.49 us
    reshape x2, local copies, waits for them, and re-layouts, real_form(): parts = block.reshape(block.shape[:-1] + (2, L, L))  9.42 us
    squeeze x2, local copies, waits for them, and re-layouts, real_form(): imag_part = parts[..., 1, :, :]  7.6 us
    unnamed x26, local copies, waits for them, and re-layouts  4.99 us
    gather x1, local copies, waits for them, and re-layouts, body(): g_real = real_form(struct_table[:, pairs])  3.39 us

profile of v1, /device:TPU:0, one launch (start us, length us, event | category | flops | bytes accessed | tf_op | source)
XLA Modules:
  0.0 100.4 jit_solution(1606972806575443180)
XLA Ops:
  0.0 0.8 slice_bitcast_fusion.6
  0.8 0.1 add.205
  0.9 0.1 add.200
  1.0 0.1 reshape.652
  1.1 2.2 %gather_fusion.2 = s32[72]{0:T(128)S(1)} fusion(s32[2,384]{1,0:T(2,128)} %param.14, s32[72]{0:T(128)S(1)} %reshape.652), kind=kCustom, calls=%fused_computation.4 | custom fusion | bytes 1152 | tf_op jit(solution)/shard_map/jit(take_along_axis)/gather | solution.py:22
  3.3 0.1 reshape.655
  3.4 0.1 add.198
  3.7 0.1 add.215
  3.9 0.1 add.217
  4.1 9.7 %gather_fusion.4 = s32[516]{0:T(1024)S(1)} fusion(s32[2,384]{1,0:T(2,128)} %param.13, s32[516]{0:T(1024)S(1)} %reshape.682), kind=kCustom, calls=%fused_computation.clone | custom fusion | bytes 8256 | tf_op jit(solution)/shard_map/jit(take_along_axis)/gather | solution.py:22
  13.9 7.5 %gather_fusion.5 = s32[516]{0:T(1024)S(1)} fusion(s32[2,384]{1,0:T(2,128)S(1)} %copy-done.1, s32[516]{0:T(1024)S(1)} %reshape.682), kind=kCustom, calls=%fused_computation.1.clone | custom fusion | bytes 8256 | tf_op jit(solution)/shard_map/jit(take_along_axis)/gather | solution.py:22
  21.6 0.1 reshape.614
  21.7 0.1 reshape.608
  21.8 0.1 reshape.646
  22.0 3.4 %gather_fusion.1 = bf16[516,2048]{1,0:T(8,128)(2,1)S(1)} fusion(bf16[64,2048]{1,0:T(8,128)(2,1)S(1)} %bitcast.108, s32[1024]{0:T(1024)S(1)} %pad_clamp_fusion), kind=kCustom, calls=%fused_computation.3 | custom fusion | bytes 4229136 | tf_op jit(solution)/shard_map/gather | solution.py:46
  25.4 9.3 %reshape.609 = bf16[1,2,43,6,2,32,32]{6,5,4,3,2,1,0:T(8,128)(2,1)} reshape(bf16[516,2048]{1,0:T(8,128)(2,1)S(1)} %gather_fusion.1) | data formatting | bytes 4227072 | tf_op jit(solution)/shard_map/reshape | solution.py:12
  34.7 7.3 %slice_bitcast_fusion = (bf16[1,2,43,6,32,32]{5,4,3,2,1,0:T(8,128)(2,1)}, bf16[1,2,43,6,32,32]{5,4,3,2,1,0:T(8,128)(2,1)}) fusion(bf16[1,2,43,6,2,32,32]{6,5,4,3,2,1,0:T(8,128)(2,1)} %reshape.609), kind=kLoop, calls=%fused_computation.14 | loop fusion | bytes 4227072 | tf_op jit(solution)/shard_map/squeeze | solution.py:14
  42.1 1.5 %copy-done.3 = bf16[1,2,43,6,2,32,32]{6,5,4,3,2,1,0:T(8,128)(2,1)S(1)} copy-done((bf16[1,2,43,6,2,32,32]{6,5,4,3,2,1,0:T(8,128)(2,1)S(1)}, bf16[1,2,43,6,2,32,32]{6,5,4,3,2,1,0:T(8,128)(2,1)}, u32[]{:S(2)}) %copy-start.3) | copy-done | bytes 2113560
  43.6 2.5 %fusion.70 = bf16[1,2,43,6,32,32]{5,4,3,2,1,0:T(8,128)(2,1)} fusion(bf16[1,2,43,6,2,32,32]{6,5,4,3,2,1,0:T(8,128)(2,1)S(1)} %copy-done.3), kind=kLoop, calls=%fused_computation.115 | loop fusion | flops 528384 | bytes 2113536 | tf_op jit(solution)/shard_map/neg | solution.py:15
  46.1 0.1 reshape.616
  46.2 0.1 copy.45
  46.3 0.1 copy.44
  46.4 0.1 convert_bitcast_fusion
  46.5 9.5 %select_reduce_fusion = bf16[2,36,64,32]{2,3,1,0:T(8,128)(2,1)S(1)} fusion(pred[2,36,6]{2,1,0:T(8,128)(4,1)S(1)} %slice_compare_fusion, bf16[1,2,43,6,32,32]{5,4,3,2,1,0:T(8,128)(2,1)} %get-tuple-element.13, bf16[1,2,43,6,32,32]{5,4,3,2,1,0:T(8,128)(2,1)} %get-tuple-element.12, bf16[1,2,43,6,32,32]{5,4,3,2,1,0:T(8,128)(2,1)} %fusion.70, ...), kind=kOutput, calls=%fused_computation.13 | convolution fusion | flops 129024000 | bytes 3473840 | tf_op jit(solution)/shard_map/easkij,eajc->easkic/dot_general | solution.py:51
  56.0 0.1 shift-left_or_fusion
  56.1 0.1 reshape.658
  56.2 2.0 %gather_fusion.3 = s32[86]{0:T(128)S(1)} fusion(s32[2,64]{1,0:T(2,128)S(1)} %copy-done.2, s32[86]{0:T(128)S(1)} %reshape.658), kind=kCustom, calls=%fused_computation.5 | custom fusion | bytes 1376 | tf_op jit(solution)/shard_map/jit(take_along_axis)/gather | solution.py:22
  58.2 0.1 gather.23
  58.3 0.1 reshape.636
  58.4 10.7 %all_gather.3 = bf16[1,16,2048]{2,0,1:T(2,128)(2,1)S(1)} all-gather(bf16[1,2,2048]{2,0,1:T(2,128)(2,1)S(1)} %copy.27), channel_id=1, replica_groups=mesh['energy'=4,'atom'=8] {'atom'}, dimensions={1}, use_global_device_ids=true | all-gather | bytes 73728 | tf_op jit(solution)/shard_map/all_gather | solution.py:27
  69.1 0.8 gather_fusion
  69.9 1.1 %reshape.694 = bf16[1,2,43,2,32,32]{5,4,3,2,1,0:T(8,128)(2,1)S(1)} reshape(bf16[86,2048]{1,0:T(8,128)(2,1)S(1)} %gather_fusion) | data formatting | bytes 704512 | tf_op jit(solution)/shard_map/gather | solution.py:43
  71.1 0.2 copy_select_fusion
  71.3 0.3 slice_bitcast_fusion.2
  71.6 0.1 fusion.69
  71.7 0.1 add_compare_fusion
  71.8 0.9 fusion.8
  72.8 0.6 copy-done.5
  73.3 1.3 %slice-done.1 = s8[4194304]{0:T(1024)(128)(4,1)S(1)} async-done(((s8[4227072]{0:T(1024)(128)(4,1)}), s8[4194304]{0:T(1024)(128)(4,1)S(1)}, s32[]{:S(2)}) %slice-start.1) | async-done | bytes 4194328
  74.7 1.3 %copy-done.4 = bf16[1,2,43,6,32,32]{5,4,3,2,1,0:T(8,128)(2,1)S(1)} copy-done((bf16[1,2,43,6,32,32]{5,4,3,2,1,0:T(8,128)(2,1)S(1)}, bf16[1,2,43,6,32,32]{5,4,3,2,1,0:T(8,128)(2,1)}, u32[]{:S(2)}) %copy-start.4) | copy-done | bytes 1056792
  75.9 0.8 fusion.23
  76.8 1.5 %fusion.27 = bf16[2,64,32]{1,2,0:T(8,128)(2,1)S(1)} fusion(bf16[2,6,64,32]{2,3,1,0:T(8,128)(2,1)S(1)} %fusion.23, bf16[1,2,43,32,32]{4,3,2,1,0:T(8,128)(2,1)S(1)} %get-tuple-element.15, bf16[1,2,43,32,32]{4,3,2,1,0:T(8,128)(2,1)S(1)} %get-tuple-element.14, bf16[1,2,43,32,32]{4,3,2,1,0:T(8,128)(2,1)S(1)} %fusion.69, ...), kind=kOutput, calls=%fused_computation.41 | convolution fusion | flops 7155712 | bytes 3772428 | tf_op jit(solution)/shard_map/eanij,eanjc->eaic/dot_general | solution.py:71
  78.2 0.2 fusion.26
  78.5 0.6 fusion.73
  79.1 1.4 %multiply_subtract_fusion = (f32[1,2,32,32]{2,3,1,0:T(8,128)S(1)}, f32[1,2,32,32]{2,3,1,0:T(8,128)S(1)}) fusion(f32[1,2,64,32]{2,3,1,0:T(8,128)S(1)} %fusion.26, f32[]{:T(128)} %bitcast.32, f32[]{:T(128)} %bitcast), kind=kLoop, calls=%fused_computation.75 | loop fusion | flops 12288 | bytes 32776 | tf_op jit(solution)/shard_map/sub | solution.py:82
  80.5 0.1 add.226
  80.7 0.1 sub.10
  80.8 19.6 %psum.7 = f32[2,2048]{1,0:T(2,128)} all-reduce(f32[2,2048]{1,0:T(2,128)S(1)} %pad_maximum_fusion.8), channel_id=1, replica_groups=mesh['energy'=4,'atom'=8] {'energy'}, use_global_device_ids=true, to_apply=%region_1.0 | all-reduce | flops 4096 | bytes 32768 | tf_op jit(solution)/shard_map/psum | solution.py:85
  (48 shorter events, 1.1 us)
Async XLA Ops:
  0.0 22.0 %copy-start = (bf16[1,64,2048]{2,1,0:T(8,128)(2,1)S(1)}, bf16[1,64,2048]{2,1,0:T(8,128)(2,1)}, u32[]{:S(2)}) copy-start(bf16[1,64,2048]{2,1,0:T(8,128)(2,1)} %param.10) | copy-start | bytes 786436
  0.0 13.9 %copy-start.1 = (s32[2,384]{1,0:T(2,128)S(1)}, s32[2,384]{1,0:T(2,128)}, u32[]{:S(2)}) copy-start(s32[2,384]{1,0:T(2,128)} %param.14) | copy-start | bytes 9220
  34.7 8.9 %copy-start.3 = (bf16[1,2,43,6,2,32,32]{6,5,4,3,2,1,0:T(8,128)(2,1)S(1)}, bf16[1,2,43,6,2,32,32]{6,5,4,3,2,1,0:T(8,128)(2,1)}, u32[]{:S(2)}) copy-start(bf16[1,2,43,6,2,32,32]{6,5,4,3,2,1,0:T(8,128)(2,1)} %reshape.609) | copy-start | bytes 6340612
  43.6 2.5 %copy-start.6 = (bf16[1,2,2048]{2,1,0:T(2,128)(2,1)S(1)}, bf16[1,2,2048]{2,1,0:T(2,128)(2,1)}, u32[]{:S(2)}) copy-start(bf16[1,2,2048]{2,1,0:T(2,128)(2,1)} %param.9) | copy-start | bytes 24580
  46.5 9.7 %copy-start.2 = (s32[2,64]{1,0:T(2,128)S(1)}, s32[2,64]{1,0:T(2,128)}, u32[]{:S(2)}) copy-start(s32[2,64]{1,0:T(2,128)} %param.11) | copy-start | bytes 1540
  56.0 15.1 %copy-start.8 = (s32[2]{0:T(128)S(1)}, s32[2]{0:T(128)}, u32[]{:S(2)}) copy-start(s32[2]{0:T(128)} %param.12) | copy-start | bytes 28
  69.9 2.8 %slice-start = ((s8[4227072]{0:T(1024)(128)(4,1)}), s8[32768]{0:T(1024)(128)(4,1)S(1)}, s32[]{:S(2)}) async-start(s8[4227072]{0:T(1024)(128)(4,1)} %bitcast.110), calls=%async_computation | async-start | bytes 65536
  71.1 2.2 %copy-start.5 = (bf16[1,2,43,6,32,32]{5,4,3,2,1,0:T(8,128)(2,1)S(1)}, bf16[1,2,43,6,32,32]{5,4,3,2,1,0:T(8,128)(2,1)}, u32[]{:S(2)}) copy-start(bf16[1,2,43,6,32,32]{5,4,3,2,1,0:T(8,128)(2,1)} %get-tuple-element.13) | copy-start | bytes 3170308
  71.3 3.3 %slice-start.1 = ((s8[4227072]{0:T(1024)(128)(4,1)}), s8[4194304]{0:T(1024)(128)(4,1)S(1)}, s32[]{:S(2)}) async-start(s8[4227072]{0:T(1024)(128)(4,1)} %bitcast.110), calls=%async_computation.1 | async-start | bytes 8388608
  71.6 4.3 %copy-start.4 = (bf16[1,2,43,6,32,32]{5,4,3,2,1,0:T(8,128)(2,1)S(1)}, bf16[1,2,43,6,32,32]{5,4,3,2,1,0:T(8,128)(2,1)}, u32[]{:S(2)}) copy-start(bf16[1,2,43,6,32,32]{5,4,3,2,1,0:T(8,128)(2,1)} %get-tuple-element.12) | copy-start | bytes 3170308
  76.8 1.7 %copy-start.7 = (f32[1,2]{1,0:T(1,128)S(1)}, f32[1,2]{1,0:T(1,128)}, u32[]{:S(2)}) copy-start(f32[1,2]{1,0:T(1,128)} %param.15) | copy-start | bytes 28

commit v2 on v0

v2 whole, which is shorter than its diff:
```python
import jax
import jax.numpy as jnp
from jax import lax
from jax.experimental import pallas as pl
from jax.experimental.pallas import tpu as pltpu
from jax.sharding import PartitionSpec as P

L = 32
Z = 64
NB = 6


def real_form(block):
    parts = block.reshape(block.shape[:-1] + (2, L, L))
    real_part = parts[..., 0, :, :]
    imag_part = parts[..., 1, :, :]
    top_rows = jnp.concatenate([real_part, -imag_part], axis=-1)
    bottom_rows = jnp.concatenate([imag_part, real_part], axis=-1)
    return jnp.concatenate([top_rows, bottom_rows], axis=-2)


def zone_kernel(links, pairs, atoms, sizes, tab, tw, out, q, near2, near3):
    a_dev = out.shape[0]
    zl = L * 2
    n1 = NB * NB

    def block(ref, index):
        return ref[pl.ds(pl.multiple_of(index * zl, zl), zl), :]

    def dot(a, b):
        return jnp.dot(a, b, preferred_element_type=jnp.float32)

    for g in range(a_dev):
        base = g * Z * NB
        size = sizes[g]
        own = atoms[g * Z]
        start_b = block(tw, own)[:, :L]
        start_f = start_b.astype(jnp.float32)
        q[...] = dot(tab[...], start_b)

        def sweep1(i, carry):
            m = i // NB
            n = i - m * NB
            slot = links[base + links[base + m] * NB + n]
            acc = jnp.zeros((zl, L), jnp.float32)
            for k in range(NB):
                spot = base + slot * NB + k
                acc = acc + jnp.where(links[spot] == 0, block(q, pairs[spot]), 0.0)
            col = jnp.where(slot < size, dot(block(tw, atoms[g * Z + slot]), acc.astype(jnp.bfloat16)), 0.0)
            col = col + jnp.where(slot == 0, start_f, 0.0)
            near2[pl.ds(pl.multiple_of(i * zl, zl), zl), :] = col.astype(jnp.bfloat16)
            return carry

        lax.fori_loop(0, n1, sweep1, 0)

        for m in range(NB):
            slot = links[base + m]
            acc = jnp.zeros((zl, L), jnp.float32)
            for n in range(NB):
                acc = acc + dot(block(tab, pairs[base + slot * NB + n]), block(near2, m * NB + n))
            col = jnp.where(slot < size, dot(block(tw, atoms[g * Z + slot]), acc.astype(jnp.bfloat16)), 0.0)
            col = col + jnp.where(slot == 0, start_f, 0.0)
            near3[pl.ds(m * zl, zl), :] = col.astype(jnp.bfloat16)

        acc = jnp.zeros((zl, L), jnp.float32)
        for n in range(NB):
            acc = acc + dot(block(tab, pairs[base + n]), near3[pl.ds(n * zl, zl), :])
        out[g] = dot(block(tw, own), acc.astype(jnp.bfloat16)) + start_f


def body(t_mats, struct_table, zone_atoms, zone_size, pair_index, zone_link, weights):
    e_dev, a_dev, block_flat = t_mats.shape
    window = lax.all_gather(t_mats, "atom", axis=1, tiled=True)
    n_atoms = window.shape[1]
    k_tab = struct_table.shape[1]
    tab = real_form(struct_table[0]).reshape(k_tab * 2 * L, 2 * L)
    tw = real_form(window[0]).reshape(n_atoms * 2 * L, 2 * L)
    smem = pl.BlockSpec(memory_space=pltpu.SMEM)
    vmem = pl.BlockSpec(memory_space=pltpu.VMEM)
    diagonal = pl.pallas_call(
        zone_kernel,
        out_shape=jax.ShapeDtypeStruct((a_dev, 2 * L, L), jnp.float32),
        in_specs=[smem, smem, smem, smem, vmem, vmem],
        out_specs=vmem,
        scratch_shapes=[
            pltpu.VMEM((k_tab * 2 * L, L), jnp.float32),
            pltpu.VMEM((NB * NB * 2 * L, L), jnp.bfloat16),
            pltpu.VMEM((NB * 2 * L, L), jnp.bfloat16),
        ],
    )(zone_link.reshape(-1), pair_index.reshape(-1), zone_atoms.reshape(-1), zone_size, tab, tw)[None]

    real_rows = diagonal[:, :, :L, :].reshape(e_dev, a_dev, L * L)
    imag_rows = diagonal[:, :, L:, :].reshape(e_dev, a_dev, L * L)
    w_real = weights[:, 0][:, None, None]
    w_imag = weights[:, 1][:, None, None]
    green_real = jnp.sum(w_real * real_rows - w_imag * imag_rows, axis=0)
    green_imag = jnp.sum(w_real * imag_rows + w_imag * real_rows, axis=0)
    local_green = jnp.concatenate([green_real, green_imag], axis=-1)
    return lax.psum(local_green, "energy")


def solution(mesh):
    return jax.shard_map(
        body,
        mesh=mesh,
        in_specs=(
            P("energy", "atom", None),
            P("energy", None, None),
            P("atom", None),
            P("atom"),
            P("atom", None),
            P("atom", None),
            P("energy", None),
        ),
        out_specs=P("atom", None),
        check_vma=False,
    )
```

time: 153 us -> 56.3 us (0.37)
  local copies, waits for them, and re-layouts: 63.7 us -> 6.49 us
  matrix products: 39.3 us -> 0 us
  other arithmetic: 19.4 us -> 3.61 us
  Pallas kernels: 0 us -> 15.5 us
    dot_general x6 -> x0, matrix products: 39.3 us -> none  [the longest x3 35.7 us: scatter_terms(): jnp.einsum(pattern, couplings, gathered, preferred_element_type=jnp.float32)]
    gather x10 -> x0, local copies, waits for them, and re-layouts: 28.5 us -> none  [the longest x5 21.5 us: take_links(): member_col[:, member_links]]
    another operation x5 -> x1, local copies, waits for them, and re-layouts: 15.9 us -> 0.19 us  [real_form(): parts = block.reshape(block.shape[:-1] + (2, L, L))]
    pallas_call x0 -> x1, Pallas kernels: none -> 15.5 us  [body(): pl.pallas_call(zone_kernel, out_shape=jax.ShapeDtypeStruct((a_dev, 2 * L,...]
    reshape x1 -> x3, local copies, waits for them, and re-layouts: 11.6 us -> 1.85 us  [the longest x1 0.66 us: body(): zone_atoms.reshape(-1)]
    add x3 -> x0, other arithmetic: 5.8 us -> none  [scatter_terms(): imag_part = products[..., 1, 0, :, :] + products[..., 0, 1, :, :]]
    sub x3 -> x0, other arithmetic: 5.49 us -> none  [scatter_terms(): real_part = products[..., 0, 0, :, :] - products[..., 1, 1, :, :]]
    convert_element_type x2 -> x0, other arithmetic: 4.6 us -> none  [solve_zones(): column_parts = column.astype(jnp.bfloat16).reshape(e_dev, a_dev, Z, 2, L, L)]
where the time goes in v2:
time: 56.3 us; the launch traced here: 56 us
  blocking collectives  30.3 us (54%)
  Pallas kernels  15.5 us (28%)
  local copies, waits for them, and re-layouts  6.49 us (12%)
  other arithmetic  3.61 us (6%)
    psum x1, blocking collectives, body(): return lax.psum(local_green, 'energy')  19.6 us
    pallas_call x1, Pallas kernels, body(): pl.pallas_call(zone_kernel, out_shape=jax.ShapeDtypeStruct((a_dev, 2 * L,...  15.5 us
    all_gather x1, blocking collectives, body(): window = lax.all_gather(t_mats, 'atom', axis=1, tiled=True)  10.7 us
    concatenate x1, local copies, waits for them, and re-layouts, real_form(): return jnp.concatenate([top_rows, bottom_rows], axis=-2)  2.35 us
    sub x1, other arithmetic, body(): green_real = jnp.sum(w_real * real_rows - w_imag * imag_rows, axis=0)  2.04 us
    unnamed x12, local copies, waits for them, and re-layouts  1.27 us
    concatenate x2, other arithmetic, real_form(): return jnp.concatenate([top_rows, bottom_rows], axis=-2)  1.14 us

profile of v2, /device:TPU:0, one launch (start us, length us, event | category | flops | bytes accessed | tf_op | source)
XLA Modules:
  0.0 56.0 jit_solution(15592220023083750617)
XLA Ops:
  0.0 1.2 %copy.21 = bf16[1,64,2048]{1,2,0:T(8,128)(2,1)S(1)} copy(bf16[1,64,2048]{2,1,0:T(8,128)(2,1)} %param.8) | data formatting | bytes 524288 | tf_op args[1]
  1.3 0.3 maximum_maximum_fusion
  1.6 0.0 copy-start
  1.6 2.4 %copy.22 = bf16[64,64,64]{2,1,0:T(8,128)(2,1)} copy(bf16[64,64,64]{0,2,1:T(8,128)(2,1)S(1)} %maximum_maximum_fusion) | data formatting | bytes 1048576 | tf_op jit(solution)/shard_map/concatenate | solution.py:19
  4.0 0.0 copy-done
  4.0 0.0 copy-start.1
  4.0 0.0 copy-start.2
  4.0 0.0 copy-start.4
  4.0 10.7 %all_gather.3 = bf16[1,16,2048]{2,0,1:T(2,128)(2,1)S(1)} all-gather(bf16[1,2,2048]{2,0,1:T(2,128)(2,1)S(1)} %copy.23), channel_id=1, replica_groups=mesh['energy'=4,'atom'=8] {'atom'}, dimensions={1}, use_global_device_ids=true | all-gather | bytes 73728 | tf_op jit(solution)/shard_map/all_gather | solution.py:73
  14.7 0.4 reduce
  15.1 0.2 reshape_squeeze.7
  15.3 0.0 copy-start.3
  15.3 0.9 %maximum_maximum_fusion.1 = bf16[16,64,64]{2,1,0:T(8,128)(2,1)} fusion(bf16[16,32,32]{2,1,0:T(8,128)(2,1)S(1)} %get-tuple-element.8, bf16[16,32,32]{2,1,0:T(8,128)(2,1)S(1)} %get-tuple-element.7, bf16[16,32,32]{2,1,0:T(8,128)(2,1)S(1)} %fusion), kind=kLoop, calls=%fused_computation.3 | loop fusion | flops 524288 | bytes 229376 | tf_op jit(solution)/shard_map/concatenate | solution.py:19
  16.2 0.0 copy-done.1
  16.2 0.6 %reshape.53.links = s32[768]{0:T(1024)} reshape(s32[2,384]{1,0:T(2,128)S(1)} %copy-done.1) | data formatting | bytes 6144 | tf_op jit(solution)/shard_map/reshape | solution.py:90
  16.8 0.0 copy-done.2
  16.8 0.6 %reshape.54.pairs = s32[768]{0:T(1024)} reshape(s32[2,384]{1,0:T(2,128)S(1)} %copy-done.2) | data formatting | bytes 6144 | tf_op jit(solution)/shard_map/reshape | solution.py:90
  17.4 0.0 copy-done.4
  17.4 0.7 %reshape.55.atoms = s32[128]{0:T(128)} reshape(s32[2,64]{1,0:T(2,128)S(1)} %copy-done.4) | data formatting | bytes 1024 | tf_op jit(solution)/shard_map/reshape | solution.py:90
  18.0 15.5 %shard_map.73 = f32[2,64,32]{2,1,0:T(8,128)} custom-call(s32[768]{0:T(1024)} %reshape.53.links, s32[768]{0:T(1024)} %reshape.54.pairs, s32[128]{0:T(128)} %reshape.55.atoms, s32[2]{0:T(128)} %sizes.1, bf16[4096,64]{1,0:T(8,128)(2,1)} %bitcast.24, bf16[1024,64]{1,0:T(8,128)(2,1)} %bitcast.27), custom_call_target="tpu_custom_call" | custom-call | tf_op jit(solution)/shard_map/pallas_call | solution.py:80
  33.6 0.0 copy-done.3
  33.6 0.6 %fusion.2 = (f32[1,1]{1,0:T(1,128)}, f32[1,1]{1,0:T(1,128)}) fusion(f32[1,2]{1,0:T(1,128)S(1)} %copy-done.3), kind=kLoop, calls=%fused_computation.11 | loop fusion | bytes 16 | tf_op jit(solution)/shard_map/slice | solution.py:94
  34.2 2.0 %multiply_subtract_fusion = (f32[1,2,32,32]{3,2,1,0:T(8,128)S(1)}, f32[1,2,32,32]{3,2,1,0:T(8,128)S(1)}) fusion(f32[1,2,64,32]{3,2,1,0:T(8,128)} %bitcast.28, f32[]{:T(128)} %bitcast.9, f32[]{:T(128)} %bitcast), kind=kLoop, calls=%fused_computation.7 | loop fusion | flops 12288 | bytes 32776 | tf_op jit(solution)/shard_map/sub | solution.py:96
  36.2 0.1 add.12
  36.3 0.1 sub.10
  36.4 19.6 %psum.7 = f32[2,2048]{1,0:T(2,128)} all-reduce(f32[2,2048]{1,0:T(2,128)S(1)} %pad_maximum_fusion), channel_id=1, replica_groups=mesh['energy'=4,'atom'=8] {'energy'}, use_global_device_ids=true, to_apply=%region_0.0 | all-reduce | flops 4096 | bytes 32768 | tf_op jit(solution)/shard_map/psum | solution.py:99
  (6 shorter events, 0.1 us)
Async XLA Ops:
  1.6 2.4 %copy-start = (bf16[1,2,2048]{2,1,0:T(2,128)(2,1)S(1)}, bf16[1,2,2048]{2,1,0:T(2,128)(2,1)}, u32[]{:S(2)}) copy-start(bf16[1,2,2048]{2,1,0:T(2,128)(2,1)} %param.7) | copy-start | bytes 24580
  4.0 12.2 %copy-start.1 = (s32[2,384]{1,0:T(2,128)S(1)}, s32[2,384]{1,0:T(2,128)}, u32[]{:S(2)}) copy-start(s32[2,384]{1,0:T(2,128)} %param.12) | copy-start | bytes 9220
  4.0 12.8 %copy-start.2 = (s32[2,384]{1,0:T(2,128)S(1)}, s32[2,384]{1,0:T(2,128)}, u32[]{:S(2)}) copy-start(s32[2,384]{1,0:T(2,128)} %param.11) | copy-start | bytes 9220
  4.0 13.4 %copy-start.4 = (s32[2,64]{1,0:T(2,128)S(1)}, s32[2,64]{1,0:T(2,128)}, u32[]{:S(2)}) copy-start(s32[2,64]{1,0:T(2,128)} %param.9) | copy-start | bytes 1540
  15.3 18.3 %copy-start.3 = (f32[1,2]{1,0:T(1,128)S(1)}, f32[1,2]{1,0:T(1,128)}, u32[]{:S(2)}) copy-start(f32[1,2]{1,0:T(1,128)} %param.13) | copy-start | bytes 28

commit v3 on v2

v3 whole, which is shorter than its diff:
```python
import functools

import jax
import jax.numpy as jnp
from jax import lax
from jax.experimental import pallas as pl
from jax.experimental.pallas import tpu as pltpu
from jax.sharding import PartitionSpec as P

L = 32
Z = 64
NB = 6


def real_form(block):
    parts = block.reshape(block.shape[:-1] + (2, L, L))
    real_part = parts[..., 0, :, :]
    imag_part = parts[..., 1, :, :]
    top_rows = jnp.concatenate([real_part, -imag_part], axis=-1)
    bottom_rows = jnp.concatenate([imag_part, real_part], axis=-1)
    return jnp.concatenate([top_rows, bottom_rows], axis=-2)


def zone_kernel(links, pairs, atoms, sizes, wts, tab, tw, out, near2, near3, acc, flags):
    a_dev = out.shape[0]
    zl = L * 2
    n1 = NB * NB

    def rows(index):
        return pl.ds(pl.multiple_of(index * zl, zl), zl)

    def dot(a, b):
        return jnp.dot(a, b, preferred_element_type=jnp.float32)

    for g in range(a_dev):
        size = sizes[g]
        own = atoms[g, 0]
        start_b = tw[rows(own), :][:, :L]
        start_f = start_b.astype(jnp.float32)

        def finish(slot, index, dest):
            live = slot < size

            @pl.when(live)
            def _():
                col = dot(tw[rows(atoms[g, slot]), :], acc[...].astype(jnp.bfloat16))
                col = col + jnp.where(slot == 0, start_f, 0.0)
                dest[rows(index), :] = col.astype(jnp.bfloat16)

            @pl.when(jnp.logical_not(live))
            def _():
                dest[rows(index), :] = jnp.zeros((zl, L), jnp.bfloat16)

        def sweep1(i, carry):
            m = i // NB
            slot = links[g, links[g, m] * NB + i - m * NB]
            hits = jnp.int32(0)
            for k in range(NB):
                hits = hits + (links[g, slot * NB + k] == 0).astype(jnp.int32)
            live = hits > 0
            flags[i] = jnp.logical_or(live, slot == 0).astype(jnp.int32)

            @pl.when(live)
            def _():
                acc[...] = jnp.zeros((zl, L), jnp.float32)
                for k in range(NB):
                    spot = slot * NB + k

                    @pl.when(links[g, spot] == 0)
                    def _():
                        acc[...] += dot(tab[rows(pairs[g, spot]), :], start_b)

                finish(slot, i, near2)

            @pl.when(jnp.logical_not(live))
            def _():
                near2[rows(i), :] = jnp.where(slot == 0, start_b, jnp.zeros((), jnp.bfloat16))

            return carry

        lax.fori_loop(0, n1, sweep1, 0)

        for m in range(NB):
            slot = links[g, m]
            acc[...] = jnp.zeros((zl, L), jnp.float32)
            live = jnp.int32(0)
            for n in range(NB):
                i = m * NB + n

                @pl.when(flags[i] != 0)
                def _():
                    acc[...] += dot(tab[rows(pairs[g, slot * NB + n]), :], near2[rows(i), :])

                live = live | flags[i]
            flags[n1 + m] = jnp.logical_or(live != 0, slot == 0).astype(jnp.int32)

            @pl.when(live != 0)
            def _():
                finish(slot, m, near3)

            @pl.when(live == 0)
            def _():
                near3[rows(m), :] = jnp.where(slot == 0, start_b, jnp.zeros((), jnp.bfloat16))

        acc[...] = jnp.zeros((zl, L), jnp.float32)
        for n in range(NB):

            @pl.when(flags[n1 + n] != 0)
            def _():
                acc[...] += dot(tab[rows(pairs[g, n]), :], near3[rows(n), :])

        col = dot(tw[rows(own), :], acc[...].astype(jnp.bfloat16)) + start_f
        w_real = wts[0, 0]
        w_imag = wts[0, 1]
        out[g, :L, :] = w_real * col[:L] - w_imag * col[L:]
        out[g, L:, :] = w_real * col[L:] + w_imag * col[:L]


def xor_pairs(n, bit):
    return [(i, i ^ bit) for i in range(n)]


def gather_atoms(t_mats, n_axis):
    if n_axis & (n_axis - 1):
        return lax.all_gather(t_mats, "atom", axis=1, tiled=True)
    index = lax.axis_index("atom")
    blocks = t_mats
    bit = 1
    while bit < n_axis:
        other = lax.ppermute(blocks, "atom", xor_pairs(n_axis, bit))
        low = (index & bit) == 0
        blocks = jnp.where(
            low, jnp.concatenate([blocks, other], axis=1), jnp.concatenate([other, blocks], axis=1)
        )
        bit *= 2
    return blocks


def sum_energies(x, n_axis):
    if n_axis & (n_axis - 1):
        return lax.psum(x, "energy")
    bit = 1
    while bit < n_axis:
        x = x + lax.ppermute(x, "energy", xor_pairs(n_axis, bit))
        bit *= 2
    return x


def body(axis_sizes, t_mats, struct_table, zone_atoms, zone_size, pair_index, zone_link, weights):
    e_dev, a_dev, block_flat = t_mats.shape
    window = gather_atoms(t_mats, axis_sizes["atom"])
    n_atoms = window.shape[1]
    k_tab = struct_table.shape[1]
    tab = real_form(struct_table[0]).reshape(k_tab * 2 * L, 2 * L)
    tw = real_form(window[0]).reshape(n_atoms * 2 * L, 2 * L)
    smem = pl.BlockSpec(memory_space=pltpu.SMEM)
    vmem = pl.BlockSpec(memory_space=pltpu.VMEM)
    blocks = pl.pallas_call(
        zone_kernel,
        out_shape=jax.ShapeDtypeStruct((a_dev, 2 * L, L), jnp.float32),
        in_specs=[smem, smem, smem, smem, smem, vmem, vmem],
        out_specs=vmem,
        scratch_shapes=[
            pltpu.VMEM((NB * NB * 2 * L, L), jnp.bfloat16),
            pltpu.VMEM((NB * 2 * L, L), jnp.bfloat16),
            pltpu.VMEM((2 * L, L), jnp.float32),
            pltpu.SMEM((NB * NB + NB,), jnp.int32),
        ],
    )(zone_link, pair_index, zone_atoms, zone_size, weights, tab, tw)
    blocks = sum_energies(blocks, axis_sizes["energy"])
    return blocks.reshape(a_dev, 2, L * L).reshape(a_dev, 2 * L * L)


def solution(mesh):
    return jax.shard_map(
        functools.partial(body, dict(mesh.shape)),
        mesh=mesh,
        in_specs=(
            P("energy", "atom", None),
            P("energy", None, None),
            P("atom", None),
            P("atom"),
            P("atom", None),
            P("atom", None),
            P("energy", None),
        ),
        out_specs=P("atom", None),
        check_vma=False,
    )
```

time: 56.3 us -> 38.4 us (0.68)
  the two profiles are of different devices: /device:TPU:0 before, /device:TPU:30 now
where the time goes in v3:
time: 38.4 us; the launch traced here: 38.2 us
  waiting for transfers between devices  15.7 us (41%)
  Pallas kernels  12.8 us (33%)
  local copies, waits for them, and re-layouts  5.18 us (13%)
  other arithmetic  2.33 us (6%)
  starting transfers between devices  2 us (5%)
    pallas_call x1, Pallas kernels, body(): pl.pallas_call(zone_kernel, out_shape=jax.ShapeDtypeStruct((a_dev, 2 * L,...  12.8 us
    ppermute x2, waiting for transfers between devices, sum_energies(): x = x + lax.ppermute(x, 'energy', xor_pairs(n_axis, bit))  9.46 us
    ppermute x3, waiting for transfers between devices, gather_atoms(): other = lax.ppermute(blocks, 'atom', xor_pairs(n_axis, bit))  6.27 us
    concatenate x1, local copies, waits for them, and re-layouts, real_form(): return jnp.concatenate([top_rows, bottom_rows], axis=-2)  2.38 us
    unnamed x3, local copies, waits for them, and re-layouts  1.62 us
    ppermute x3, starting transfers between devices, gather_atoms(): other = lax.ppermute(blocks, 'atom', xor_pairs(n_axis, bit))  1.17 us
    concatenate x2, other arithmetic, real_form(): return jnp.concatenate([top_rows, bottom_rows], axis=-2)  1.16 us
    add x2, other arithmetic, sum_energies(): x = x + lax.ppermute(x, 'energy', xor_pairs(n_axis, bit))  0.86 us
  transfers between devices with their start and end apart: 5, of which 4 were waited for; matrix products, arithmetic and copies ran while one was open for 11% of the time, Pallas kernels for 0%

profile of v3, /device:TPU:30, one launch (start us, length us, event | category | flops | bytes accessed | tf_op | source)
XLA Modules:
  0.0 38.2 jit_solution(1247184718927837057)
XLA Ops:
  0.0 0.0 collective-permute-start
  0.0 1.2 %copy.18 = bf16[1,64,2048]{1,2,0:T(8,128)(2,1)S(1)} copy(bf16[1,64,2048]{2,1,0:T(8,128)(2,1)} %param.8) | data formatting | bytes 524288 | tf_op args[1]
  1.3 0.0 copy-start
  1.3 0.3 maximum_maximum_fusion
  1.6 0.4 %copy-done = bf16[1,2,2048]{2,1,0:T(2,128)(2,1)S(1)} copy-done((bf16[1,2,2048]{2,1,0:T(2,128)(2,1)S(1)}, bf16[1,2,2048]{2,1,0:T(2,128)(2,1)}, u32[]{:S(2)}) %copy-start) | copy-done | bytes 8216
  2.0 0.1 concatenate.133
  2.1 2.4 %copy.19 = bf16[64,64,64]{2,1,0:T(8,128)(2,1)} copy(bf16[64,64,64]{0,2,1:T(8,128)(2,1)S(1)} %maximum_maximum_fusion) | data formatting | bytes 1048576 | tf_op jit(solution)/shard_map/concatenate | solution.py:21
  4.5 0.0 collective-permute-done
  4.5 0.6 %collective-permute-start.1 = (bf16[1,4,2048]{2,1,0:T(4,128)(2,1)S(1)}, bf16[1,4,2048]{2,1,0:T(4,128)(2,1)S(1)}, u32[]{:S(2)}, u32[]{:S(2)}) collective-permute-start(bf16[1,4,2048]{2,1,0:T(4,128)(2,1)S(1)} %maximum_select_fusion.3), channel_id=1, source_target_pairs={{0,2},{1,3},{2,0},{3,1},{4,6},{5,7},{6,4},{7,5},{8,10},{9,11},{10,... | collective-permute-start | bytes 49160 | tf_op jit(solution)/shard_map/ppermute | solution.py:130
  5.1 0.1 concatenate.134
  5.3 3.0 %collective-permute-done.1 = bf16[1,4,2048]{2,1,0:T(4,128)(2,1)S(1)} collective-permute-done((bf16[1,4,2048]{2,1,0:T(4,128)(2,1)S(1)}, bf16[1,4,2048]{2,1,0:T(4,128)(2,1)S(1)}, u32[]{:S(2)}, u32[]{:S(2)}) %collective-permute-start.1) | collective-permute-done | bytes 16416 | tf_op jit(solution)/shard_map/ppermute | solution.py:130
  8.4 0.6 %collective-permute-start.2 = (bf16[1,8,2048]{2,1,0:T(8,128)(2,1)S(1)}, bf16[1,8,2048]{2,1,0:T(8,128)(2,1)S(1)}, u32[]{:S(2)}, u32[]{:S(2)}) collective-permute-start(bf16[1,8,2048]{2,1,0:T(8,128)(2,1)S(1)} %maximum_select_fusion.2), channel_id=1, source_target_pairs={{0,4},{1,5},{2,6},{3,7},{4,0},{5,1},{6,2},{7,3},{8,12},{9,13},{10,... | collective-permute-start | bytes 98312 | tf_op jit(solution)/shard_map/ppermute | solution.py:130
  8.9 0.1 concatenate.139
  9.1 3.2 %collective-permute-done.2 = bf16[1,8,2048]{2,1,0:T(8,128)(2,1)S(1)} collective-permute-done((bf16[1,8,2048]{2,1,0:T(8,128)(2,1)S(1)}, bf16[1,8,2048]{2,1,0:T(8,128)(2,1)S(1)}, u32[]{:S(2)}, u32[]{:S(2)}) %collective-permute-start.2) | collective-permute-done | bytes 32800 | tf_op jit(solution)/shard_map/ppermute | solution.py:130
  12.4 0.1 concatenate.149
  12.5 0.1 maximum_select_fusion
  12.7 0.9 %maximum_maximum_fusion.1 = bf16[16,64,64]{2,1,0:T(8,128)(2,1)} fusion(bf16[16,32,32]{2,1,0:T(8,128)(2,1)S(1)} %get-tuple-element.8, bf16[16,32,32]{2,1,0:T(8,128)(2,1)S(1)} %get-tuple-element.7, bf16[16,32,32]{2,1,0:T(8,128)(2,1)S(1)} %fusion.1), kind=kLoop, calls=%fused_computation.4 | loop fusion | flops 524288 | bytes 229376 | tf_op jit(solution)/shard_map/concatenate | solution.py:21
  13.5 12.8 %shard_map.73 = f32[2,64,32]{2,1,0:T(8,128)} custom-call(s32[2,384]{1,0:T(2,128)} %links.1, s32[2,384]{1,0:T(2,128)} %pairs.1, s32[2,64]{1,0:T(2,128)} %atoms.1, s32[2]{0:T(128)} %sizes.1, f32[1,2]{1,0:T(1,128)} %wts.1, bf16[4096,64]{1,0:T(8,128)(2,1)} %bitcast.19, bf16[1024,64]{1,0:T(8,128)(2,1)} %bitcast.22), custom_call_target="tpu_custom_call" | custom-call | tf_op jit(solution)/shard_map/pallas_call | solution.py:158
  26.3 0.4 %collective-permute-start.3 = (f32[2,64,32]{2,1,0:T(8,128)}, f32[2,64,32]{2,1,0:T(8,128)S(1)}, u32[]{:S(2)}, u32[]{:S(2)}) collective-permute-start(f32[2,64,32]{2,1,0:T(8,128)} %shard_map.73), channel_id=1, source_target_pairs={{0,8},{8,0},{16,24},{24,16},{1,9},{9,1},{17,25},{25,17},{2,10},{10... | collective-permute-start | bytes 49160 | tf_op jit(solution)/shard_map/ppermute | solution.py:144
  26.8 4.6 %collective-permute-done.3 = f32[2,64,32]{2,1,0:T(8,128)S(1)} collective-permute-done((f32[2,64,32]{2,1,0:T(8,128)}, f32[2,64,32]{2,1,0:T(8,128)S(1)}, u32[]{:S(2)}, u32[]{:S(2)}) %collective-permute-start.3) | collective-permute-done | bytes 16416 | tf_op jit(solution)/shard_map/ppermute | solution.py:144
  31.4 0.9 %add.6 = f32[2,64,32]{2,1,0:T(8,128)S(1)} add(f32[2,64,32]{2,1,0:T(8,128)} %shard_map.73, f32[2,64,32]{2,1,0:T(8,128)S(1)} %collective-permute-done.3) | non-fusion elementwise | flops 4096 | bytes 49152 | tf_op jit(solution)/shard_map/add | solution.py:144
  32.2 0.4 collective-permute-start.4
  32.6 4.9 %collective-permute-done.4 = f32[2,64,32]{2,1,0:T(8,128)S(1)} collective-permute-done((f32[2,64,32]{2,1,0:T(8,128)S(1)}, f32[2,64,32]{2,1,0:T(8,128)S(1)}, u32[]{:S(2)}, u32[]{:S(2)}) %collective-permute-start.4) | collective-permute-done | bytes 16416 | tf_op jit(solution)/shard_map/ppermute | solution.py:144
  37.5 0.7 %reshape_reshape.3 = f32[2,2048]{1,0:T(2,128)} reshape(f32[2,64,32]{2,1,0:T(8,128)S(1)} %add.7) | data formatting | bytes 32768 | tf_op jit(solution)/shard_map/reshape;reshape | solution.py:171
  (11 shorter events, 0.3 us)
Async XLA Ops:
  0.0 4.5 %collective-permute-start = (bf16[1,2,2048]{2,1,0:T(2,128)(2,1)}, bf16[1,2,2048]{2,1,0:T(2,128)(2,1)S(1)}, u32[]{:S(2)}, u32[]{:S(2)}) collective-permute-start(bf16[1,2,2048]{2,1,0:T(2,128)(2,1)} %param.7), channel_id=1, source_target_pairs={{0,1},{1,0},{2,3},{3,2},{4,5},{5,4},{6,7},{7,6},{8,9},{9,8},{10,11... | collective-permute-start | bytes 24584 | tf_op jit(solution)/shard_map/ppermute | solution.py:130
  1.3 0.7 %copy-start = (bf16[1,2,2048]{2,1,0:T(2,128)(2,1)S(1)}, bf16[1,2,2048]{2,1,0:T(2,128)(2,1)}, u32[]{:S(2)}) copy-start(bf16[1,2,2048]{2,1,0:T(2,128)(2,1)} %param.7) | copy-start | bytes 24580
  4.5 3.8 %collective-permute-start.1 = (bf16[1,4,2048]{2,1,0:T(4,128)(2,1)S(1)}, bf16[1,4,2048]{2,1,0:T(4,128)(2,1)S(1)}, u32[]{:S(2)}, u32[]{:S(2)}) collective-permute-start(bf16[1,4,2048]{2,1,0:T(4,128)(2,1)S(1)} %maximum_select_fusion.3), channel_id=1, source_target_pairs={{0,2},{1,3},{2,0},{3,1},{4,6},{5,7},{6,4},{7,5},{8,10},{9,11},{10,... | collective-permute-start | bytes 49160 | tf_op jit(solution)/shard_map/ppermute | solution.py:130
  8.4 4.0 %collective-permute-start.2 = (bf16[1,8,2048]{2,1,0:T(8,128)(2,1)S(1)}, bf16[1,8,2048]{2,1,0:T(8,128)(2,1)S(1)}, u32[]{:S(2)}, u32[]{:S(2)}) collective-permute-start(bf16[1,8,2048]{2,1,0:T(8,128)(2,1)S(1)} %maximum_select_fusion.2), channel_id=1, source_target_pairs={{0,4},{1,5},{2,6},{3,7},{4,0},{5,1},{6,2},{7,3},{8,12},{9,13},{10,... | collective-permute-start | bytes 98312 | tf_op jit(solution)/shard_map/ppermute | solution.py:130
  26.3 5.1 %collective-permute-start.3 = (f32[2,64,32]{2,1,0:T(8,128)}, f32[2,64,32]{2,1,0:T(8,128)S(1)}, u32[]{:S(2)}, u32[]{:S(2)}) collective-permute-start(f32[2,64,32]{2,1,0:T(8,128)} %shard_map.73), channel_id=1, source_target_pairs={{0,8},{8,0},{16,24},{24,16},{1,9},{9,1},{17,25},{25,17},{2,10},{10... | collective-permute-start | bytes 49160 | tf_op jit(solution)/shard_map/ppermute | solution.py:144
  32.2 5.2 %collective-permute-start.4 = (f32[2,64,32]{2,1,0:T(8,128)S(1)}, f32[2,64,32]{2,1,0:T(8,128)S(1)}, u32[]{:S(2)}, u32[]{:S(2)}) collective-permute-start(f32[2,64,32]{2,1,0:T(8,128)S(1)} %add.6), channel_id=1, source_target_pairs={{0,16},{8,24},{16,0},{24,8},{1,17},{9,25},{17,1},{25,9},{2,18},{10... | collective-permute-start | bytes 49160 | tf_op jit(solution)/shard_map/ppermute | solution.py:144
